TPU v7x, 256 devices: a whole 4x4x8 slice. The times are simulated.
256 devices in a mesh: hyp: 32 (over y, x, core), head: 8 (over z).
Axes of the slice: x: 4, y: 4, z: 8, core: 2. Of those that a mesh axis runs over, the one named last changes fastest.
Arguments:
- step_embeds: bfloat16 [3, 512, 4096], P(None, 'hyp'), may hold values from -6 to 6
- lang_table: bfloat16 [8, 4096], replicated, may hold values from -3 to 3
- lang_ids: int32 [32, 4], replicated, may hold values from 0 to 7
- self_gain: float32 [4096], replicated, may hold values from 0.1 to 1.9
- self_wq: bfloat16 [4096, 2048], P(None, 'head'), may hold values from -0.09375 to 0.09375
- self_wk: bfloat16 [4096, 2048], P(None, 'head'), may hold values from -0.09375 to 0.09375
- self_wv: bfloat16 [4096, 2048], P(None, 'head'), may hold values from -0.09375 to 0.09375
- self_wo: bfloat16 [2048, 4096], P('head'), may hold values from -0.125 to 0.125
- cross_gain: float32 [4096], replicated, may hold values from 0.1 to 1.9
- cross_wq: bfloat16 [4096, 2048], P(None, 'head'), may hold values from -0.09375 to 0.09375
- cross_wkv: bfloat16 [4096, 4096], P('hyp', 'head'), may hold values from -0.09375 to 0.09375
- encoder_rows: bfloat16 [24576, 4096], P('hyp', 'head'), may hold values from -200 to 200
- doc_lengths: int32 [32], P('hyp'), may hold values from 192 to 768, as said below
- past_keys: bfloat16 [512, 32, 2048], P('hyp', None, 'head'), may hold values from -200 to 200
- past_values: bfloat16 [512, 32, 2048], P('hyp', None, 'head'), may hold values from -6 to 6
- parents: int32 [3, 512], replicated, may hold values from 0 to 3
Outputs:
- cross_context: bfloat16 [3, 512, 2048], P(None, 'hyp', 'head')
- final_keys: bfloat16 [512, 35, 2048], P('hyp', None, 'head')
- final_values: bfloat16 [512, 35, 2048], P('hyp', None, 'head')
Inputs may be any that keep to these rules, and one draw needn't show every extreme that they name: `doc_lengths`: some document has exactly 768 live rows. `parents`: A parent is a beam of the same document and target.
All inputs are finite; a program needn't handle non-finite values.
Results may differ from a plain program's by a relative error of at most 0.03.
Values may be sent and summed in bfloat16 or wider, within the bound.
No kernel may reach another device: no remote copies, remote signals or barrier semaphores. Data moves between devices by JAX's collectives and lax.ppermute only.
A program may use at most 128 MiB of HBM per device.

v0:
```python
import jax
import jax.numpy as jnp
from jax import lax
from jax.sharding import PartitionSpec as P

HEAD = 256
BEAMS = 4
TARGETS = 4
STEPS = 3
EPSILON = 1e-06


def rms_scaled(values_in, gain):
    mean_square = jnp.mean(values_in * values_in, axis=-1, keepdims=True)
    return values_in * lax.rsqrt(mean_square + EPSILON) * gain


def pick_rows(candidates, selector, row_axis):
    shape_list = [1] * candidates[0].ndim
    shape_list[row_axis] = selector.shape[0]
    chosen = candidates[0]
    for position in range(1, len(candidates)):
        chosen = jnp.where((selector == position).reshape(shape_list), candidates[position], chosen)
    return chosen


def beam_copies(block, hyp_count, group_size):
    copies = [block]
    for hop in range(1, BEAMS):
        distance = hop * group_size
        route = [((i - distance) % hyp_count, i) for i in range(hyp_count)]
        copies.append(lax.ppermute(block, "hyp", route))
    return copies


def cross_attend(queries, cross_keys, cross_values, doc_length, scaling):
    scores = (
        jnp.einsum("qd,jd->qj", queries, cross_keys, preferred_element_type=jnp.float32) * scaling
    )
    live_mask = lax.broadcasted_iota(jnp.int32, (1, cross_keys.shape[0]), 1) < doc_length
    scores = jnp.where(live_mask, scores, -jnp.inf)
    highest = jnp.max(scores, axis=1, keepdims=True)
    raw_weights = jnp.exp(scores - highest)
    totals = jnp.sum(raw_weights, axis=1, keepdims=True)
    weights = (raw_weights / totals).astype(jnp.bfloat16)
    output = jnp.einsum("qj,jd->qd", weights, cross_values, preferred_element_type=jnp.float32)
    return output.astype(jnp.bfloat16)


def shards(
    step_embeds,
    lang_table,
    lang_ids,
    self_gain,
    self_wq,
    self_wk,
    self_wv,
    self_wo,
    cross_gain,
    cross_wq,
    cross_wkv,
    encoder_rows,
    doc_lengths,
    past_keys,
    past_values,
    parents,
):
    hyp_count = lax.axis_size("hyp")
    group_size = hyp_count // BEAMS
    my_index = lax.axis_index("hyp")
    my_beam = my_index // group_size
    my_slot = my_index % group_size
    steps = step_embeds.shape[0]
    row_count = step_embeds.shape[1]
    docs_here = row_count // TARGETS
    head_width = self_wq.shape[1]
    doc_count = lang_ids.shape[0]
    past_len = past_keys.shape[1]
    scaling = HEAD ** (-0.5)
    full_weights = lax.all_gather(cross_wkv, "hyp", axis=0, tiled=True)
    full_rows = lax.all_gather(encoder_rows, "head", axis=1, tiled=True)
    cross_kv = jnp.dot(full_rows, full_weights, preferred_element_type=jnp.float32).astype(
        jnp.bfloat16
    )
    cross_kv = cross_kv.reshape(encoder_rows.shape[0], 2, HEAD)
    cross_keys = cross_kv[:, 0, :]
    cross_values = cross_kv[:, 1, :]
    doc_length = doc_lengths[0]
    past_stack = jnp.stack([past_keys, past_values])
    past_all = beam_copies(past_stack, hyp_count, group_size)
    my_langs = lax.dynamic_slice_in_dim(lang_ids, my_slot * docs_here, docs_here, 0).reshape(
        row_count
    )
    one_hot = (
        my_langs[:, None] == lax.broadcasted_iota(jnp.int32, (1, lang_table.shape[0]), 1)
    ).astype(jnp.bfloat16)
    lang_rows = jnp.dot(one_hot, lang_table, preferred_element_type=jnp.float32)
    hidden_in = step_embeds.astype(jnp.float32) + lang_rows[None]
    normed = rms_scaled(hidden_in, self_gain).astype(jnp.bfloat16).reshape(steps * row_count, -1)
    new_query = jnp.dot(normed, self_wq, preferred_element_type=jnp.float32).astype(jnp.bfloat16)
    new_key = jnp.dot(normed, self_wk, preferred_element_type=jnp.float32).astype(jnp.bfloat16)
    new_value = jnp.dot(normed, self_wv, preferred_element_type=jnp.float32).astype(jnp.bfloat16)
    new_query = new_query.reshape(steps, row_count, head_width)
    fresh = jnp.stack([new_key, new_value]).reshape(2, steps, row_count, head_width)
    fresh_all = beam_copies(fresh, hyp_count, group_size)
    parent_view = parents.reshape(steps, BEAMS, doc_count * TARGETS)
    parent_of = lax.dynamic_slice_in_dim(parent_view, my_slot * row_count, row_count, 2)
    own_beam = jnp.full((row_count,), my_beam, jnp.int32)

    def hop_of(beam):
        return (my_beam - beam) % BEAMS

    def climb(step_idx, beam):
        return jnp.take_along_axis(parent_of[step_idx], beam[None, :], axis=0)[0]

    def cache_at(step_idx):
        ancestor = own_beam
        new_parts = [None] * (step_idx + 1)
        new_parts[step_idx] = fresh[:, step_idx]
        for back in range(step_idx, 0, -1):
            ancestor = climb(back, ancestor)
            new_parts[back - 1] = pick_rows(
                [f[:, back - 1] for f in fresh_all], hop_of(ancestor), 1
            )
        ancestor = climb(0, ancestor)
        past_part = pick_rows(past_all, hop_of(ancestor), 1)
        return jnp.concatenate([past_part] + [n[:, :, None, :] for n in new_parts], axis=2)

    contexts = []
    final_cache = None
    for step_idx in range(steps):
        cache = cache_at(step_idx)
        if step_idx == steps - 1:
            final_cache = cache
        query = new_query[step_idx]
        scores = (
            jnp.einsum("rd,rpd->rp", query, cache[0], preferred_element_type=jnp.float32) * scaling
        )
        highest = jnp.max(scores, axis=1, keepdims=True)
        raw_weights = jnp.exp(scores - highest)
        totals = jnp.sum(raw_weights, axis=1, keepdims=True)
        summed = jnp.einsum(
            "rp,rpd->rd",
            raw_weights,
            cache[1].astype(jnp.float32),
            preferred_element_type=jnp.float32,
        )
        contexts.append((summed / totals).astype(jnp.bfloat16))
    self_context = jnp.stack(contexts).reshape(steps * row_count, head_width)
    partial_out = jnp.dot(self_context, self_wo, preferred_element_type=jnp.float32)
    summed_out = lax.psum(partial_out.astype(jnp.bfloat16), "head").astype(jnp.float32)
    residual = hidden_in + summed_out.reshape(hidden_in.shape)
    normed_cross = rms_scaled(residual, cross_gain).astype(jnp.bfloat16)
    cross_query = jnp.dot(
        normed_cross.reshape(steps * row_count, -1), cross_wq, preferred_element_type=jnp.float32
    ).astype(jnp.bfloat16)
    by_doc = cross_query.reshape(steps, docs_here, TARGETS, head_width)
    sent = []
    for shift in range(BEAMS):
        route = [
            (beam * group_size + slot, slot * docs_here + (beam + shift) % BEAMS)
            for beam in range(BEAMS)
            for slot in range(group_size)
        ]
        piece = lax.dynamic_index_in_dim(by_doc, (my_beam + shift) % BEAMS, 1, keepdims=False)
        sent.append(lax.ppermute(piece, "hyp", route))
    doc_queries = jnp.stack(sent).reshape(BEAMS * steps * TARGETS, head_width)
    answer = cross_attend(doc_queries, cross_keys, cross_values, doc_length, scaling)
    answer = answer.reshape(BEAMS, steps, TARGETS, head_width)
    back = []
    for shift in range(BEAMS):
        route = [
            (slot * docs_here + (beam + shift) % BEAMS, beam * group_size + slot)
            for beam in range(BEAMS)
            for slot in range(group_size)
        ]
        back.append(lax.ppermute(answer[shift], "hyp", route))
    back = jnp.stack(back)
    order = (jnp.arange(docs_here, dtype=jnp.int32) - my_beam) % BEAMS
    by_k = jnp.take(back, order, axis=0)
    contexts_out = by_k.transpose(1, 0, 2, 3).reshape(steps, row_count, head_width)
    return (contexts_out, final_cache[0], final_cache[1])


def solution(mesh):
    return jax.shard_map(
        shards,
        mesh=mesh,
        in_specs=(
            P(None, "hyp", None),
            P(),
            P(),
            P(),
            P(None, "head"),
            P(None, "head"),
            P(None, "head"),
            P("head", None),
            P(),
            P(None, "head"),
            P("hyp", "head"),
            P("hyp", "head"),
            P("hyp"),
            P("hyp", None, "head"),
            P("hyp", None, "head"),
            P(),
        ),
        out_specs=(P(None, "hyp", "head"), P("hyp", None, "head"), P("hyp", None, "head")),
        check_vma=False,
    )
```

profile of v0, /device:TPU:17, one launch (start us, length us, event | category | flops | bytes accessed | tf_op | source)
XLA Modules:
  0.0 224.9 jit_solution(5241141596806689058)
XLA Ops:
  8.1 0.9 constant_dynamic-slice_fusion
  9.2 1.1 fusion.42
  10.2 1.3 multiply_reduce_fusion.1
  11.6 1.2 multiply_convert_fusion.1
  12.8 2.1 convolution_convert_fusion.4
  14.9 0.5 convolution_convert_fusion.5
  15.4 0.2 collective-permute-start.3
  15.6 2.6 %collective-permute-start.4 = (bf16[2,3,16,256]{3,2,0,1:T(8,128)(2,1)S(1)}, bf16[2,3,16,256]{3,2,0,1:T(8,128)(2,1)S(1)}, u32[]{:S(2)}, u32[]{:S(2)}) collective-permute-start(bf16[2,3,16,256]{3,2,0,1:T(8,128)(2,1)S(1)} %pad_maximum_fusion.4), channel_id=1, source_target_pairs={{128,0},{136,8},{144,16},{152,24},{160,32},{168,40},{176,48},{184,... | collective-permute-start | bytes 147464 | tf_op jit(solution)/shard_map/ppermute | solution.py:32
  18.3 0.3 copy_bitcast_fusion
  18.6 0.8 pad_maximum_fusion.2
  19.4 1.5 collective-permute-start
  20.9 1.6 collective-permute-start.1
  22.7 0.7 gather_fusion.4
  23.4 0.5 broadcast_compare_fusion.12
  23.9 0.7 gather_fusion.2
  24.6 0.5 copy-done.10
  25.1 1.2 gather_fusion.5
  26.3 0.7 fusion.61
  27.0 0.7 gather_fusion.1
  27.7 0.7 gather_fusion.3
  28.4 1.2 broadcast_compare_fusion.16
  29.6 0.5 broadcast_compare_fusion.9
  30.1 1.1 broadcast_compare_fusion.6
  31.2 0.7 gather_fusion.6
  32.0 2.1 convolution_convert_fusion.6
  34.2 0.3 collective-permute-start.2
  34.7 11.1 %collective-permute-done.2 = bf16[2,16,32,256]{3,1,2,0:T(8,128)(2,1)S(1)} collective-permute-done((bf16[2,16,32,256]{3,1,2,0:T(8,128)(2,1)}, bf16[2,16,32,256]{3,1,2,0:T(8,128)(2,1)S(1)}, u32[]{:S(2)}, u32[]{:S(2)}) %collective-permute-start.2) | collective-permute-done | bytes 524320 | tf_op jit(solution)/shard_map/ppermute | solution.py:32
  45.8 1.5 select_select_fusion.2
  47.5 0.2 fusion.3
  47.7 0.1 multiply_reduce_fusion.2
  47.8 0.2 fusion.66
  48.2 0.2 fusion.7
  48.4 0.1 multiply_reduce_fusion.3
  48.5 0.2 fusion.64
  48.7 0.2 fusion.11
  48.9 0.1 multiply_reduce_fusion.4
  49.1 0.2 fusion.63
  49.3 0.2 fusion.1
  49.6 0.2 fusion.5
  49.9 0.2 fusion.9
  50.2 1.2 convolution_convert_fusion
  51.6 0.5 all-gather.5.cloned.1.call-update
  52.1 0.5 all-gather.3.cloned.1.call-update
  53.4 78.1 %all-reduce.2.cloned.1.call-done = bf16[3,16,4096]{2,1,0:T(8,128)(2,1)} async-done(((bf16[3,16,4096]{2,1,0:T(8,128)(2,1)}), bf16[3,16,4096]{2,1,0:T(8,128)(2,1)}) %all-reduce.2.cloned.1.call-update) | async-done | bytes 393232 | tf_op jit(solution)/shard_map/psum | solution.py:151
  131.6 1.4 multiply_reduce_fusion
  133.0 1.2 multiply_convert_fusion
  134.2 0.5 convolution_convert_fusion.3
  134.7 4.6 %collective-permute-start.9 = (bf16[3,4,256]{2,1,0:T(4,128)(2,1)S(1)}, bf16[3,4,256]{2,1,0:T(4,128)(2,1)S(1)}, u32[]{:S(2)}, u32[]{:S(2)}) collective-permute-start(bf16[3,4,256]{2,1,0:T(4,128)(2,1)S(1)} %get-tuple-element.43), channel_id=1, source_target_pairs={{0,24},{8,56},{16,88},{24,120},{32,152},{40,184},{48,216},{56,248}... | collective-permute-start | bytes 18440 | tf_op jit(solution)/shard_map/ppermute | solution.py:166
  139.3 12.5 %collective-permute-start.8 = (bf16[3,4,256]{2,1,0:T(4,128)(2,1)S(1)}, bf16[3,4,256]{2,1,0:T(4,128)(2,1)S(1)}, u32[]{:S(2)}, u32[]{:S(2)}) collective-permute-start(bf16[3,4,256]{2,1,0:T(4,128)(2,1)S(1)} %get-tuple-element.44), channel_id=1, source_target_pairs={{0,16},{8,48},{16,80},{24,112},{32,144},{40,176},{48,208},{56,240}... | collective-permute-start | bytes 18440 | tf_op jit(solution)/shard_map/ppermute | solution.py:166
  151.8 5.5 %collective-permute-start.7 = (bf16[3,4,256]{2,1,0:T(4,128)(2,1)S(1)}, bf16[3,4,256]{2,1,0:T(4,128)(2,1)S(1)}, u32[]{:S(2)}, u32[]{:S(2)}) collective-permute-start(bf16[3,4,256]{2,1,0:T(4,128)(2,1)S(1)} %get-tuple-element.45), channel_id=1, source_target_pairs={{0,8},{8,40},{16,72},{24,104},{32,136},{40,168},{48,200},{56,232},... | collective-permute-start | bytes 18440 | tf_op jit(solution)/shard_map/ppermute | solution.py:166
  157.3 3.3 %collective-permute-start.6 = (bf16[3,4,256]{2,1,0:T(4,128)(2,1)S(1)}, bf16[3,4,256]{2,1,0:T(4,128)(2,1)S(1)}, u32[]{:S(2)}, u32[]{:S(2)}) collective-permute-start(bf16[3,4,256]{2,1,0:T(4,128)(2,1)S(1)} %get-tuple-element.42), channel_id=1, source_target_pairs={{0,0},{8,32},{16,64},{24,96},{32,128},{40,160},{48,192},{56,224},{... | collective-permute-start | bytes 18440 | tf_op jit(solution)/shard_map/ppermute | solution.py:166
  160.6 4.0 %collective-permute-done.6 = bf16[3,4,256]{2,1,0:T(4,128)(2,1)S(1)} collective-permute-done((bf16[3,4,256]{2,1,0:T(4,128)(2,1)S(1)}, bf16[3,4,256]{2,1,0:T(4,128)(2,1)S(1)}, u32[]{:S(2)}, u32[]{:S(2)}) %collective-permute-start.6) | collective-permute-done | bytes 6176 | tf_op jit(solution)/shard_map/ppermute | solution.py:166
  164.7 21.2 %all-gather.3.cloned.1.call-done = bf16[768,4096]{1,0:T(8,128)(2,1)} async-done(((bf16[768,512]{1,0:T(8,128)(2,1)}), bf16[768,4096]{1,0:T(8,128)(2,1)}) %all-gather.3.cloned.1.call-update) | async-done | bytes 6291472 | tf_op jit(solution)/shard_map/all_gather | solution.py:81
  186.0 7.5 %convolution_convert_fusion.1 = bf16[768,512]{0,1:T(8,128)(2,1)S(1)} fusion(bf16[768,4096]{1,0:T(8,128)(2,1)} %all-gather.3.cloned.1.call-done, bf16[4096,512]{1,0:T(8,128)(2,1)} %all-gather.5.cloned.1.call-done), kind=kOutput, calls=%fused_computation.8 | convolution fusion | flops 3221618688 | bytes 11272192 | tf_op jit(solution)/shard_map/dot_general | solution.py:82
  193.4 0.3 fusion.68
  193.7 0.2 fusion.16
  193.9 0.2 convolution_convert_fusion.2
  194.3 5.6 %collective-permute-start.13 = (bf16[3,4,256]{2,1,0:T(4,128)(2,1)S(1)}, bf16[3,4,256]{2,1,0:T(4,128)(2,1)S(1)}, u32[]{:S(2)}, u32[]{:S(2)}) collective-permute-start(bf16[3,4,256]{2,1,0:T(4,128)(2,1)S(1)} %squeeze.124), channel_id=1, source_target_pairs={{24,0},{56,8},{88,16},{120,24},{152,32},{184,40},{216,48},{248,56}... | collective-permute-start | bytes 18440 | tf_op jit(solution)/shard_map/ppermute | solution.py:177
  199.9 1.7 collective-permute-start.12
  201.7 5.9 %collective-permute-start.11 = (bf16[3,4,256]{2,1,0:T(4,128)(2,1)S(1)}, bf16[3,4,256]{2,1,0:T(4,128)(2,1)S(1)}, u32[]{:S(2)}, u32[]{:S(2)}) collective-permute-start(bf16[3,4,256]{2,1,0:T(4,128)(2,1)S(1)} %squeeze.122), channel_id=1, source_target_pairs={{8,0},{40,8},{72,16},{104,24},{136,32},{168,40},{200,48},{232,56},... | collective-permute-start | bytes 18440 | tf_op jit(solution)/shard_map/ppermute | solution.py:177
  207.6 2.9 %collective-permute-start.10 = (bf16[3,4,256]{2,1,0:T(4,128)(2,1)S(1)}, bf16[3,4,256]{2,1,0:T(4,128)(2,1)S(1)}, u32[]{:S(2)}, u32[]{:S(2)}) collective-permute-start(bf16[3,4,256]{2,1,0:T(4,128)(2,1)S(1)} %squeeze.121), channel_id=1, source_target_pairs={{0,0},{32,8},{64,16},{96,24},{128,32},{160,40},{192,48},{224,56},{... | collective-permute-start | bytes 18440 | tf_op jit(solution)/shard_map/ppermute | solution.py:177
  210.6 5.6 %collective-permute-done.10 = bf16[3,4,256]{2,1,0:T(4,128)(2,1)S(1)} collective-permute-done((bf16[3,4,256]{2,1,0:T(4,128)(2,1)S(1)}, bf16[3,4,256]{2,1,0:T(4,128)(2,1)S(1)}, u32[]{:S(2)}, u32[]{:S(2)}) %collective-permute-start.10) | collective-permute-done | bytes 6176 | tf_op jit(solution)/shard_map/ppermute | solution.py:177
  216.2 0.6 gather_fusion
  216.9 0.6 reshape.460
  (100 shorter events, 2.0 us)
Async XLA Ops:
  8.0 42.2 %copy-start = (bf16[256,4096]{1,0:T(8,128)(2,1)S(1)}, bf16[256,4096]{1,0:T(8,128)(2,1)}, u32[]{:S(2)}) copy-start(bf16[256,4096]{1,0:T(8,128)(2,1)} %param.25) | copy-start | bytes 6291460
  8.0 123.5 %all-reduce.2.cloned.1.call-start = ((), (), s32[]{:S(2)}) async-start(), calls=%async_computation | async-start | bytes 786432 | tf_op jit(solution)/shard_map/psum | solution.py:151
  10.2 4.7 %copy-start.2 = (bf16[4096,256]{1,0:T(8,128)(2,1)S(1)}, bf16[4096,256]{1,0:T(8,128)(2,1)}, u32[]{:S(2)}) copy-start(bf16[4096,256]{1,0:T(8,128)(2,1)} %param.23) | copy-start | bytes 6291460
  12.7 5.5 %copy-start.6 = (bf16[16,32,256]{2,1,0:T(8,128)(2,1)S(1)}, bf16[16,32,256]{2,1,0:T(8,128)(2,1)}, u32[]{:S(2)}) copy-start(bf16[16,32,256]{2,1,0:T(8,128)(2,1)} %param.32) | copy-start | bytes 786436
  12.7 5.5 %copy-start.7 = (bf16[16,32,256]{2,1,0:T(8,128)(2,1)S(1)}, bf16[16,32,256]{2,1,0:T(8,128)(2,1)}, u32[]{:S(2)}) copy-start(bf16[16,32,256]{2,1,0:T(8,128)(2,1)} %param.31) | copy-start | bytes 786436
  14.9 7.5 %copy-start.9 = (s32[3,512]{1,0:T(4,128)S(1)}, s32[3,512]{1,0:T(4,128)}, u32[]{:S(2)}) copy-start(s32[3,512]{1,0:T(4,128)} %param.33) | copy-start | bytes 18436
  15.4 18.8 %collective-permute-start.3 = (bf16[2,3,16,256]{3,2,0,1:T(8,128)(2,1)S(1)}, bf16[2,3,16,256]{3,2,0,1:T(8,128)(2,1)S(1)}, u32[]{:S(2)}, u32[]{:S(2)}) collective-permute-start(bf16[2,3,16,256]{3,2,0,1:T(8,128)(2,1)S(1)} %pad_maximum_fusion.4), channel_id=1, source_target_pairs={{64,0},{72,8},{80,16},{88,24},{96,32},{104,40},{112,48},{120,56},{... | collective-permute-start | bytes 147464 | tf_op jit(solution)/shard_map/ppermute | solution.py:32
  15.6 18.8 %collective-permute-start.4 = (bf16[2,3,16,256]{3,2,0,1:T(8,128)(2,1)S(1)}, bf16[2,3,16,256]{3,2,0,1:T(8,128)(2,1)S(1)}, u32[]{:S(2)}, u32[]{:S(2)}) collective-permute-start(bf16[2,3,16,256]{3,2,0,1:T(8,128)(2,1)S(1)} %pad_maximum_fusion.4), channel_id=1, source_target_pairs={{128,0},{136,8},{144,16},{152,24},{160,32},{168,40},{176,48},{184,... | collective-permute-start | bytes 147464 | tf_op jit(solution)/shard_map/ppermute | solution.py:32
  18.3 16.2 %collective-permute-start.5 = (bf16[2,3,16,256]{3,2,0,1:T(8,128)(2,1)S(1)}, bf16[2,3,16,256]{3,2,0,1:T(8,128)(2,1)S(1)}, u32[]{:S(2)}, u32[]{:S(2)}) collective-permute-start(bf16[2,3,16,256]{3,2,0,1:T(8,128)(2,1)S(1)} %pad_maximum_fusion.4), channel_id=1, source_target_pairs={{192,0},{200,8},{208,16},{216,24},{224,32},{232,40},{240,48},{248,... | collective-permute-start | bytes 147464 | tf_op jit(solution)/shard_map/ppermute | solution.py:32
  19.4 15.3 %collective-permute-start = (bf16[2,16,32,256]{3,1,2,0:T(8,128)(2,1)}, bf16[2,16,32,256]{3,1,2,0:T(8,128)(2,1)}, u32[]{:S(2)}, u32[]{:S(2)}) collective-permute-start(bf16[2,16,32,256]{3,1,2,0:T(8,128)(2,1)} %pad_maximum_fusion.2), channel_id=1, source_target_pairs={{64,0},{72,8},{80,16},{88,24},{96,32},{104,40},{112,48},{120,56},{... | collective-permute-start | bytes 1572872 | tf_op jit(solution)/shard_map/ppermute | solution.py:32
  20.9 13.8 %collective-permute-start.1 = (bf16[2,16,32,256]{3,1,2,0:T(8,128)(2,1)}, bf16[2,16,32,256]{3,1,2,0:T(8,128)(2,1)}, u32[]{:S(2)}, u32[]{:S(2)}) collective-permute-start(bf16[2,16,32,256]{3,1,2,0:T(8,128)(2,1)} %pad_maximum_fusion.2), channel_id=1, source_target_pairs={{128,0},{136,8},{144,16},{152,24},{160,32},{168,40},{176,48},{184,... | collective-permute-start | bytes 1572872 | tf_op jit(solution)/shard_map/ppermute | solution.py:32
  24.6 0.5 copy-start.10
  31.9 2.2 copy-start.15
  31.9 2.6 %copy-start.11 = (pred[16]{0:T(512)(128)(4,1)S(1)}, pred[16]{0:T(512)(128)(4,1)}, u32[]{:S(2)}) copy-start(pred[16]{0:T(512)(128)(4,1)} %get-tuple-element.66) | copy-start | bytes 52
  31.9 2.6 %copy-start.12 = (pred[16]{0:T(512)(128)(4,1)S(1)}, pred[16]{0:T(512)(128)(4,1)}, u32[]{:S(2)}) copy-start(pred[16]{0:T(512)(128)(4,1)} %get-tuple-element.67) | copy-start | bytes 52
  31.9 2.6 %copy-start.13 = (pred[16]{0:T(512)(128)(4,1)S(1)}, pred[16]{0:T(512)(128)(4,1)}, u32[]{:S(2)}) copy-start(pred[16]{0:T(512)(128)(4,1)} %get-tuple-element.68) | copy-start | bytes 52
  31.9 2.6 %copy-start.14 = (pred[16]{0:T(512)(128)(4,1)S(1)}, pred[16]{0:T(512)(128)(4,1)}, u32[]{:S(2)}) copy-start(pred[16]{0:T(512)(128)(4,1)} %get-tuple-element.69) | copy-start | bytes 52
  34.2 11.7 %collective-permute-start.2 = (bf16[2,16,32,256]{3,1,2,0:T(8,128)(2,1)}, bf16[2,16,32,256]{3,1,2,0:T(8,128)(2,1)S(1)}, u32[]{:S(2)}, u32[]{:S(2)}) collective-permute-start(bf16[2,16,32,256]{3,1,2,0:T(8,128)(2,1)} %pad_maximum_fusion.2), channel_id=1, source_target_pairs={{192,0},{200,8},{208,16},{216,24},{224,32},{232,40},{240,48},{248,... | collective-permute-start | bytes 1572872 | tf_op jit(solution)/shard_map/ppermute | solution.py:32
  47.5 1.2 copy-start.5
  47.5 1.8 copy-start.4
  50.1 81.4 %copy-start.1 = (bf16[3,16,4096]{2,1,0:T(8,128)(2,1)S(1)}, bf16[3,16,4096]{2,1,0:T(8,128)(2,1)}, u32[]{:S(2)}) copy-start(bf16[3,16,4096]{2,1,0:T(8,128)(2,1)} %param.18) | copy-start | bytes 1179652
  50.2 82.7 %copy-start.8 = (f32[4096]{0:T(1024)S(1)}, f32[4096]{0:T(1024)}, u32[]{:S(2)}) copy-start(f32[4096]{0:T(1024)} %param.26) | copy-start | bytes 49156
  51.5 113.2 %all-gather.5.cloned.1.call-start = ((), (), s32[]{:S(2)}) async-start(), calls=%async_computation.2 | async-start | bytes 4325376 | tf_op jit(solution)/shard_map/all_gather | solution.py:80
  52.1 133.9 %all-gather.3.cloned.1.call-start = ((), (), s32[]{:S(2)}) async-start(), calls=%async_computation.1 | async-start | bytes 7077888 | tf_op jit(solution)/shard_map/all_gather | solution.py:81
  131.6 2.6 %copy-start.3 = (bf16[4096,256]{1,0:T(8,128)(2,1)S(1)}, bf16[4096,256]{1,0:T(8,128)(2,1)}, u32[]{:S(2)}) copy-start(bf16[4096,256]{1,0:T(8,128)(2,1)} %param.27) | copy-start | bytes 6291460
  134.7 25.9 %collective-permute-start.9 = (bf16[3,4,256]{2,1,0:T(4,128)(2,1)S(1)}, bf16[3,4,256]{2,1,0:T(4,128)(2,1)S(1)}, u32[]{:S(2)}, u32[]{:S(2)}) collective-permute-start(bf16[3,4,256]{2,1,0:T(4,128)(2,1)S(1)} %get-tuple-element.43), channel_id=1, source_target_pairs={{0,24},{8,56},{16,88},{24,120},{32,152},{40,184},{48,216},{56,248}... | collective-permute-start | bytes 18440 | tf_op jit(solution)/shard_map/ppermute | solution.py:166
  139.3 21.3 %collective-permute-start.8 = (bf16[3,4,256]{2,1,0:T(4,128)(2,1)S(1)}, bf16[3,4,256]{2,1,0:T(4,128)(2,1)S(1)}, u32[]{:S(2)}, u32[]{:S(2)}) collective-permute-start(bf16[3,4,256]{2,1,0:T(4,128)(2,1)S(1)} %get-tuple-element.44), channel_id=1, source_target_pairs={{0,16},{8,48},{16,80},{24,112},{32,144},{40,176},{48,208},{56,240}... | collective-permute-start | bytes 18440 | tf_op jit(solution)/shard_map/ppermute | solution.py:166
  151.8 8.8 %collective-permute-start.7 = (bf16[3,4,256]{2,1,0:T(4,128)(2,1)S(1)}, bf16[3,4,256]{2,1,0:T(4,128)(2,1)S(1)}, u32[]{:S(2)}, u32[]{:S(2)}) collective-permute-start(bf16[3,4,256]{2,1,0:T(4,128)(2,1)S(1)} %get-tuple-element.45), channel_id=1, source_target_pairs={{0,8},{8,40},{16,72},{24,104},{32,136},{40,168},{48,200},{56,232},... | collective-permute-start | bytes 18440 | tf_op jit(solution)/shard_map/ppermute | solution.py:166
  157.3 7.4 %collective-permute-start.6 = (bf16[3,4,256]{2,1,0:T(4,128)(2,1)S(1)}, bf16[3,4,256]{2,1,0:T(4,128)(2,1)S(1)}, u32[]{:S(2)}, u32[]{:S(2)}) collective-permute-start(bf16[3,4,256]{2,1,0:T(4,128)(2,1)S(1)} %get-tuple-element.42), channel_id=1, source_target_pairs={{0,0},{8,32},{16,64},{24,96},{32,128},{40,160},{48,192},{56,224},{... | collective-permute-start | bytes 18440 | tf_op jit(solution)/shard_map/ppermute | solution.py:166
  194.3 16.3 %collective-permute-start.13 = (bf16[3,4,256]{2,1,0:T(4,128)(2,1)S(1)}, bf16[3,4,256]{2,1,0:T(4,128)(2,1)S(1)}, u32[]{:S(2)}, u32[]{:S(2)}) collective-permute-start(bf16[3,4,256]{2,1,0:T(4,128)(2,1)S(1)} %squeeze.124), channel_id=1, source_target_pairs={{24,0},{56,8},{88,16},{120,24},{152,32},{184,40},{216,48},{248,56}... | collective-permute-start | bytes 18440 | tf_op jit(solution)/shard_map/ppermute | solution.py:177
  199.9 10.7 %collective-permute-start.12 = (bf16[3,4,256]{2,1,0:T(4,128)(2,1)S(1)}, bf16[3,4,256]{2,1,0:T(4,128)(2,1)S(1)}, u32[]{:S(2)}, u32[]{:S(2)}) collective-permute-start(bf16[3,4,256]{2,1,0:T(4,128)(2,1)S(1)} %squeeze.123), channel_id=1, source_target_pairs={{16,0},{48,8},{80,16},{112,24},{144,32},{176,40},{208,48},{240,56}... | collective-permute-start | bytes 18440 | tf_op jit(solution)/shard_map/ppermute | solution.py:177
  201.7 8.9 %collective-permute-start.11 = (bf16[3,4,256]{2,1,0:T(4,128)(2,1)S(1)}, bf16[3,4,256]{2,1,0:T(4,128)(2,1)S(1)}, u32[]{:S(2)}, u32[]{:S(2)}) collective-permute-start(bf16[3,4,256]{2,1,0:T(4,128)(2,1)S(1)} %squeeze.122), channel_id=1, source_target_pairs={{8,0},{40,8},{72,16},{104,24},{136,32},{168,40},{200,48},{232,56},... | collective-permute-start | bytes 18440 | tf_op jit(solution)/shard_map/ppermute | solution.py:177
  207.6 8.6 %collective-permute-start.10 = (bf16[3,4,256]{2,1,0:T(4,128)(2,1)S(1)}, bf16[3,4,256]{2,1,0:T(4,128)(2,1)S(1)}, u32[]{:S(2)}, u32[]{:S(2)}) collective-permute-start(bf16[3,4,256]{2,1,0:T(4,128)(2,1)S(1)} %squeeze.121), channel_id=1, source_target_pairs={{0,0},{32,8},{64,16},{96,24},{128,32},{160,40},{192,48},{224,56},{... | collective-permute-start | bytes 18440 | tf_op jit(solution)/shard_map/ppermute | solution.py:177
Sparse Core Ops, SparseCore 0:
  51.6 79.8 all-reduce.1
Sparse Core Ops, SparseCore 1:
  54.5 55.5 all-gather.4
  111.8 74.1 all-gather.2
where the time goes:
time: 225 us
  waiting for transfers between devices  121 us (54%)
  starting transfers between devices  48.4 us (22%)
  between operations  16.9 us (8%)
  matrix products  16.7 us (7%)
  other arithmetic  13.6 us (6%)
  local copies, waits for them, and re-layouts  8.23 us (4%)
    psum x1, waiting for transfers between devices, shards(): lax.psum(partial_out.astype(jnp.bfloat16), 'head').astype(jnp.float32)  78.1 us
    ppermute x4, starting transfers between devices, shards(): sent.append(lax.ppermute(piece, 'hyp', route))  25.9 us
    all_gather x1, waiting for transfers between devices, shards(): full_rows = lax.all_gather(encoder_rows, 'head', axis=1, tiled=True)  21.2 us
    ppermute x4, starting transfers between devices, shards(): back.append(lax.ppermute(answer[shift], 'hyp', route))  16.2 us
    ppermute x6, waiting for transfers between devices, beam_copies(): copies.append(lax.ppermute(block, 'hyp', route))  11.1 us
    dot_general x1, matrix products, shards(): jnp.dot(full_rows, full_weights, preferred_element_type=jnp.float32)  7.47 us
    ppermute x6, starting transfers between devices, beam_copies(): copies.append(lax.ppermute(block, 'hyp', route))  6.19 us
    ppermute x4, waiting for transfers between devices, shards(): back.append(lax.ppermute(answer[shift], 'hyp', route))  5.57 us
  transfers between devices with their start and end apart: 17, of which 5 were waited for; matrix products, arithmetic and copies ran while one was open for 7% of the time, Pallas kernels for 0%

commit v1 on v0

--- a/solution.py
+++ b/solution.py
@@ -1,3 +1,4 @@
+import functools
 import jax
 import jax.numpy as jnp
 from jax import lax
@@ -8,6 +9,24 @@
 TARGETS = 4
 STEPS = 3
 EPSILON = 1e-06
+
+
+def update_scenes(own_rows, mesh_name):
+    axis_total = lax.axis_size(mesh_name)
+    runs = list(map(lambda w: (w, (w + 1) % axis_total), range(axis_total)))
+    arrivals = list(map(lambda w: (w, (w - 1) % axis_total), range(axis_total)))
+    v_next, state_now = ([own_rows], [own_rows])
+    for _ in range(axis_total // 2):
+        v_next.append(lax.ppermute(v_next[-1], axis_name=mesh_name, perm=runs))
+    for _ in tuple(range((axis_total - 1) // 2)):
+        state_now.append(lax.ppermute(state_now[-1], mesh_name, arrivals))
+    step_out = jnp.concatenate([*v_next[::-1], *state_now[1:]], axis=1)
+    return jnp.roll(
+        step_out, (lax.axis_index(mesh_name) - axis_total // 2) * own_rows.shape[1], axis=1
+    )
+
+
+make_views = functools.partial(update_scenes, mesh_name="head")
 
 
 def rms_scaled(values_in, gain):
@@ -78,7 +97,7 @@
     past_len = past_keys.shape[1]
     scaling = HEAD ** (-0.5)
     full_weights = lax.all_gather(cross_wkv, "hyp", axis=0, tiled=True)
-    full_rows = lax.all_gather(encoder_rows, "head", axis=1, tiled=True)
+    full_rows = make_views(encoder_rows)
     cross_kv = jnp.dot(full_rows, full_weights, preferred_element_type=jnp.float32).astype(
         jnp.bfloat16
     )

time: 225 us -> 226 us (level)
  the two profiles are of different devices: /device:TPU:17 before, /device:TPU:14 now
where the time goes in v1:
time: 226 us; the launch traced here: 225 us
  waiting for transfers between devices  83.1 us (37%)
  starting transfers between devices  50.5 us (22%)
  local copies, waits for them, and re-layouts  38.7 us (17%)
  matrix products  19.9 us (9%)
  between operations  16.7 us (7%)
  other arithmetic  16 us (7%)
    ppermute x4, waiting for transfers between devices, update_scenes(): v_next.append(lax.ppermute(v_next[-1], axis_name=mesh_name, perm=runs))  39.2 us
    unnamed x39, local copies, waits for them, and re-layouts  28.8 us
    psum x1, waiting for transfers between devices, shards(): lax.psum(partial_out.astype(jnp.bfloat16), 'head').astype(jnp.float32)  28.1 us
    ppermute x4, starting transfers between devices, shards(): back.append(lax.ppermute(answer[shift], 'hyp', route))  17.7 us
    ppermute x4, starting transfers between devices, shards(): sent.append(lax.ppermute(piece, 'hyp', route))  13.8 us
    ppermute x3, starting transfers between devices, update_scenes(): state_now.append(lax.ppermute(state_now[-1], mesh_name, arrivals))  8.37 us
    dot_general x1, matrix products, shards(): jnp.dot(full_rows, full_weights, preferred_element_type=jnp.float32)  7.47 us
    ppermute x6, starting transfers between devices, beam_copies(): copies.append(lax.ppermute(block, 'hyp', route))  7.04 us
  transfers between devices with their start and end apart: 23, of which 8 were waited for; matrix products, arithmetic and copies ran while one was open for 25% of the time, Pallas kernels for 0%

profile of v1, /device:TPU:14, one launch (start us, length us, event | category | flops | bytes accessed | tf_op | source)
XLA Modules:
  0.0 224.9 jit_solution(6001965818877092859)
XLA Ops:
  8.1 1.5 copy_bitcast_fusion
  10.2 0.8 pad_maximum_fusion.2
  11.5 2.6 %collective-permute-start.1 = (bf16[2,16,32,256]{3,1,2,0:T(8,128)(2,1)}, bf16[2,16,32,256]{3,1,2,0:T(8,128)(2,1)}, u32[]{:S(2)}, u32[]{:S(2)}) collective-permute-start(bf16[2,16,32,256]{3,1,2,0:T(8,128)(2,1)} %pad_maximum_fusion.2), channel_id=1, source_target_pairs={{128,0},{136,8},{144,16},{152,24},{160,32},{168,40},{176,48},{184,... | collective-permute-start | bytes 1572872 | tf_op jit(solution)/shard_map/ppermute | solution.py:51
  14.1 1.9 collective-permute-start.2
  16.0 0.8 constant_dynamic-slice_fusion.3
  16.9 1.1 fusion.47
  18.0 1.2 multiply_reduce_fusion.1
  19.2 1.2 multiply_convert_fusion.1
  20.3 2.1 convolution_convert_fusion.4
  22.5 2.1 convolution_convert_fusion.3
  25.4 1.3 collective-permute-start.4
  26.7 0.7 reshape.452
  29.6 0.7 gather_fusion.5
  30.4 0.7 gather_fusion.1
  31.1 0.7 gather_fusion.6
  33.7 2.1 convolution_convert_fusion.5
  35.8 0.7 broadcast_compare_fusion.7
  36.5 2.4 %collective-permute-done.3 = bf16[2,3,16,256]{3,2,0,1:T(8,128)(2,1)} collective-permute-done((bf16[2,3,16,256]{3,2,0,1:T(8,128)(2,1)}, bf16[2,3,16,256]{3,2,0,1:T(8,128)(2,1)}, u32[]{:S(2)}, u32[]{:S(2)}) %collective-permute-start.3) | collective-permute-done | bytes 49184 | tf_op jit(solution)/shard_map/ppermute | solution.py:51
  39.5 0.8 fusion.71
  40.2 2.9 %collective-permute-done.5 = bf16[2,3,16,256]{3,2,0,1:T(8,128)(2,1)S(1)} collective-permute-done((bf16[2,3,16,256]{3,2,0,1:T(8,128)(2,1)}, bf16[2,3,16,256]{3,2,0,1:T(8,128)(2,1)S(1)}, u32[]{:S(2)}, u32[]{:S(2)}) %collective-permute-start.5) | collective-permute-done | bytes 49184 | tf_op jit(solution)/shard_map/ppermute | solution.py:51
  43.1 0.9 fusion.40
  44.0 0.8 fusion.37
  44.9 1.8 select_select_fusion.2
  49.6 1.2 convolution_convert_fusion
  51.4 2.0 collective-permute-start.10
  53.4 21.8 %collective-permute-done.10 = bf16[768,512]{1,0:T(8,128)(2,1)S(1)} collective-permute-done((bf16[768,512]{1,0:T(8,128)(2,1)S(1)}, bf16[768,512]{1,0:T(8,128)(2,1)S(1)}, u32[]{:S(2)}, u32[]{:S(2)}) %collective-permute-start.10) | collective-permute-done | bytes 786464 | tf_op jit(solution)/shard_map/ppermute | solution.py:20
  75.2 0.9 copy-done.3
  76.1 3.2 %collective-permute-start.14 = (bf16[768,512]{1,0:T(8,128)(2,1)S(1)}, bf16[768,512]{1,0:T(8,128)(2,1)}, u32[]{:S(2)}, u32[]{:S(2)}) collective-permute-start(bf16[768,512]{1,0:T(8,128)(2,1)S(1)} %copy-done.2), channel_id=1, source_target_pairs={{0,7},{1,0},{2,1},{3,2},{4,3},{5,4},{6,5},{7,6},{8,15},{9,8},{10,9... | collective-permute-start | bytes 2359304 | tf_op jit(solution)/shard_map/ppermute | solution.py:22
  79.4 17.4 %collective-permute-done.11 = bf16[768,512]{1,0:T(8,128)(2,1)} collective-permute-done((bf16[768,512]{1,0:T(8,128)(2,1)S(1)}, bf16[768,512]{1,0:T(8,128)(2,1)}, u32[]{:S(2)}, u32[]{:S(2)}) %collective-permute-start.11) | collective-permute-done | bytes 786464 | tf_op jit(solution)/shard_map/ppermute | solution.py:20
  97.3 3.2 %collective-permute-start.15 = (bf16[768,512]{1,0:T(8,128)(2,1)}, bf16[768,512]{1,0:T(8,128)(2,1)}, u32[]{:S(2)}, u32[]{:S(2)}) collective-permute-start(bf16[768,512]{1,0:T(8,128)(2,1)} %collective-permute-done.14), channel_id=1, source_target_pairs={{0,7},{1,0},{2,1},{3,2},{4,3},{5,4},{6,5},{7,6},{8,15},{9,8},{10,9... | collective-permute-start | bytes 2359304 | tf_op jit(solution)/shard_map/ppermute | solution.py:22
  100.6 28.1 %all-reduce.2.cloned.1.call-done = bf16[3,16,4096]{2,1,0:T(8,128)(2,1)} async-done(((bf16[3,16,4096]{2,1,0:T(8,128)(2,1)}), bf16[3,16,4096]{2,1,0:T(8,128)(2,1)}) %all-reduce.2.cloned.1.call-update) | async-done | bytes 393232 | tf_op jit(solution)/shard_map/psum | solution.py:170
  128.7 1.2 multiply_reduce_fusion
  129.9 1.5 collective-permute-start.13
  131.4 1.2 multiply_convert_fusion
  132.6 2.1 convolution_convert_fusion.2
  134.7 1.9 collective-permute-start.6
  137.9 4.8 %collective-permute-start.7 = (bf16[3,4,256]{2,1,0:T(4,128)(2,1)S(1)}, bf16[3,4,256]{2,1,0:T(4,128)(2,1)S(1)}, u32[]{:S(2)}, u32[]{:S(2)}) collective-permute-start(bf16[3,4,256]{2,1,0:T(4,128)(2,1)S(1)} %get-tuple-element.45), channel_id=1, source_target_pairs={{0,8},{8,40},{16,72},{24,104},{32,136},{40,168},{48,200},{56,232},... | collective-permute-start | bytes 18440 | tf_op jit(solution)/shard_map/ppermute | solution.py:185
  142.8 2.2 collective-permute-start.8
  145.0 4.8 %collective-permute-start.9 = (bf16[3,4,256]{2,1,0:T(4,128)(2,1)S(1)}, bf16[3,4,256]{2,1,0:T(4,128)(2,1)S(1)}, u32[]{:S(2)}, u32[]{:S(2)}) collective-permute-start(bf16[3,4,256]{2,1,0:T(4,128)(2,1)S(1)} %get-tuple-element.43), channel_id=1, source_target_pairs={{0,24},{8,56},{16,88},{24,120},{32,152},{40,184},{48,216},{56,248}... | collective-permute-start | bytes 18440 | tf_op jit(solution)/shard_map/ppermute | solution.py:185
  149.8 4.0 %collective-permute-done.9 = bf16[3,4,256]{2,1,0:T(4,128)(2,1)S(1)} collective-permute-done((bf16[3,4,256]{2,1,0:T(4,128)(2,1)S(1)}, bf16[3,4,256]{2,1,0:T(4,128)(2,1)S(1)}, u32[]{:S(2)}, u32[]{:S(2)}) %collective-permute-start.9) | collective-permute-done | bytes 6176 | tf_op jit(solution)/shard_map/ppermute | solution.py:185
  153.9 1.9 collective-permute-start.16
  155.8 2.2 constant_dynamic-update-slice_fusion.15
  158.0 2.1 constant_dynamic-update-slice_fusion.14
  160.1 2.1 constant_dynamic-update-slice_fusion.13
  162.2 2.1 constant_dynamic-update-slice_fusion.12
  164.3 1.0 constant_dynamic-update-slice_fusion.11
  165.2 2.1 constant_dynamic-update-slice_fusion.10
  167.3 2.1 constant_dynamic-update-slice_fusion.9
  169.4 1.3 collective-permute-done.16
  170.8 0.9 constant_dynamic-update-slice_fusion.8
  171.7 2.1 constant_dynamic-update-slice_fusion.7
  173.8 2.2 constant_dynamic-update-slice_fusion.6
  176.0 2.1 constant_dynamic-update-slice_fusion.5
  178.1 1.0 constant_dynamic-update-slice_fusion.4
  179.1 1.0 constant_dynamic-update-slice_fusion.3
  180.1 2.1 constant_dynamic-update-slice_fusion.2
  182.2 2.1 constant_dynamic-update-slice_fusion.1
  184.3 1.0 constant_dynamic-update-slice_fusion
  185.3 7.5 %fusion.2 = bf16[768,512]{0,1:T(8,128)(2,1)S(1)} fusion(bf16[4096,512]{1,0:T(8,128)(2,1)} %all-gather.2.cloned.1.call-done, bf16[768,8192]{1,0:T(8,128)(2,1)} %constant_dynamic-update-slice_fusion, s32[]{:T(128)S(6)} %select_n.355), kind=kOutput, calls=%fused_computation.10 | convolution fusion | flops 3221618688 | bytes 11272196 | tf_op jit(solution)/shard_map/dot_general | solution.py:101
  193.6 2.3 %collective-permute-start.17 = (bf16[3,4,256]{2,1,0:T(4,128)(2,1)S(1)}, bf16[3,4,256]{2,1,0:T(4,128)(2,1)S(1)}, u32[]{:S(2)}, u32[]{:S(2)}) collective-permute-start(bf16[3,4,256]{2,1,0:T(4,128)(2,1)S(1)} %squeeze.121), channel_id=1, source_target_pairs={{0,0},{32,8},{64,16},{96,24},{128,32},{160,40},{192,48},{224,56},{... | collective-permute-start | bytes 18440 | tf_op jit(solution)/shard_map/ppermute | solution.py:196
  196.0 7.8 %collective-permute-start.18 = (bf16[3,4,256]{2,1,0:T(4,128)(2,1)S(1)}, bf16[3,4,256]{2,1,0:T(4,128)(2,1)S(1)}, u32[]{:S(2)}, u32[]{:S(2)}) collective-permute-start(bf16[3,4,256]{2,1,0:T(4,128)(2,1)S(1)} %squeeze.122), channel_id=1, source_target_pairs={{8,0},{40,8},{72,16},{104,24},{136,32},{168,40},{200,48},{232,56},... | collective-permute-start | bytes 18440 | tf_op jit(solution)/shard_map/ppermute | solution.py:196
  203.8 3.2 %collective-permute-start.19 = (bf16[3,4,256]{2,1,0:T(4,128)(2,1)S(1)}, bf16[3,4,256]{2,1,0:T(4,128)(2,1)S(1)}, u32[]{:S(2)}, u32[]{:S(2)}) collective-permute-start(bf16[3,4,256]{2,1,0:T(4,128)(2,1)S(1)} %squeeze.123), channel_id=1, source_target_pairs={{16,0},{48,8},{80,16},{112,24},{144,32},{176,40},{208,48},{240,56}... | collective-permute-start | bytes 18440 | tf_op jit(solution)/shard_map/ppermute | solution.py:196
  207.0 4.4 %collective-permute-start.20 = (bf16[3,4,256]{2,1,0:T(4,128)(2,1)S(1)}, bf16[3,4,256]{2,1,0:T(4,128)(2,1)S(1)}, u32[]{:S(2)}, u32[]{:S(2)}) collective-permute-start(bf16[3,4,256]{2,1,0:T(4,128)(2,1)S(1)} %squeeze.124), channel_id=1, source_target_pairs={{24,0},{56,8},{88,16},{120,24},{152,32},{184,40},{216,48},{248,56}... | collective-permute-start | bytes 18440 | tf_op jit(solution)/shard_map/ppermute | solution.py:196
  211.5 4.6 %collective-permute-done.20 = bf16[3,4,256]{2,1,0:T(4,128)(2,1)S(1)} collective-permute-done((bf16[3,4,256]{2,1,0:T(4,128)(2,1)S(1)}, bf16[3,4,256]{2,1,0:T(4,128)(2,1)S(1)}, u32[]{:S(2)}, u32[]{:S(2)}) %collective-permute-start.20) | collective-permute-done | bytes 6176 | tf_op jit(solution)/shard_map/ppermute | solution.py:196
  (119 shorter events, 13.9 us)
Async XLA Ops:
  8.0 41.6 %copy-start = (bf16[256,4096]{1,0:T(8,128)(2,1)S(1)}, bf16[256,4096]{1,0:T(8,128)(2,1)}, u32[]{:S(2)}) copy-start(bf16[256,4096]{1,0:T(8,128)(2,1)} %param.25) | copy-start | bytes 6291460
  8.0 120.6 %all-reduce.2.cloned.1.call-start = ((), (), s32[]{:S(2)}) async-start(), calls=%async_computation | async-start | bytes 786432 | tf_op jit(solution)/shard_map/psum | solution.py:170
  9.5 0.7 copy-start.5
  9.5 1.5 copy-start.6
  11.1 33.8 %collective-permute-start = (bf16[2,16,32,256]{3,1,2,0:T(8,128)(2,1)}, bf16[2,16,32,256]{3,1,2,0:T(8,128)(2,1)}, u32[]{:S(2)}, u32[]{:S(2)}) collective-permute-start(bf16[2,16,32,256]{3,1,2,0:T(8,128)(2,1)} %pad_maximum_fusion.2), channel_id=1, source_target_pairs={{64,0},{72,8},{80,16},{88,24},{96,32},{104,40},{112,48},{120,56},{... | collective-permute-start | bytes 1572872 | tf_op jit(solution)/shard_map/ppermute | solution.py:51
  11.5 33.4 %collective-permute-start.1 = (bf16[2,16,32,256]{3,1,2,0:T(8,128)(2,1)}, bf16[2,16,32,256]{3,1,2,0:T(8,128)(2,1)}, u32[]{:S(2)}, u32[]{:S(2)}) collective-permute-start(bf16[2,16,32,256]{3,1,2,0:T(8,128)(2,1)} %pad_maximum_fusion.2), channel_id=1, source_target_pairs={{128,0},{136,8},{144,16},{152,24},{160,32},{168,40},{176,48},{184,... | collective-permute-start | bytes 1572872 | tf_op jit(solution)/shard_map/ppermute | solution.py:51
  14.1 30.8 %collective-permute-start.2 = (bf16[2,16,32,256]{3,1,2,0:T(8,128)(2,1)}, bf16[2,16,32,256]{3,1,2,0:T(8,128)(2,1)}, u32[]{:S(2)}, u32[]{:S(2)}) collective-permute-start(bf16[2,16,32,256]{3,1,2,0:T(8,128)(2,1)} %pad_maximum_fusion.2), channel_id=1, source_target_pairs={{192,0},{200,8},{208,16},{216,24},{224,32},{232,40},{240,48},{248,... | collective-permute-start | bytes 1572872 | tf_op jit(solution)/shard_map/ppermute | solution.py:51
  22.4 2.2 copy-start.8
  22.4 106.2 %copy-start.1 = (bf16[3,16,4096]{2,1,0:T(8,128)(2,1)S(1)}, bf16[3,16,4096]{2,1,0:T(8,128)(2,1)}, u32[]{:S(2)}) copy-start(bf16[3,16,4096]{2,1,0:T(8,128)(2,1)} %param.18) | copy-start | bytes 1179652
  22.4 108.9 %copy-start.11 = (f32[4096]{0:T(1024)S(1)}, f32[4096]{0:T(1024)}, u32[]{:S(2)}) copy-start(f32[4096]{0:T(1024)} %param.26) | copy-start | bytes 49156
  24.6 0.6 copy-start.9
  25.2 13.6 %collective-permute-start.3 = (bf16[2,3,16,256]{3,2,0,1:T(8,128)(2,1)}, bf16[2,3,16,256]{3,2,0,1:T(8,128)(2,1)}, u32[]{:S(2)}, u32[]{:S(2)}) collective-permute-start(bf16[2,3,16,256]{3,2,0,1:T(8,128)(2,1)} %pad_maximum_fusion.4), channel_id=1, source_target_pairs={{64,0},{72,8},{80,16},{88,24},{96,32},{104,40},{112,48},{120,56},{... | collective-permute-start | bytes 147464 | tf_op jit(solution)/shard_map/ppermute | solution.py:51
  25.4 14.9 %collective-permute-start.4 = (bf16[2,3,16,256]{3,2,0,1:T(8,128)(2,1)}, bf16[2,3,16,256]{3,2,0,1:T(8,128)(2,1)}, u32[]{:S(2)}, u32[]{:S(2)}) collective-permute-start(bf16[2,3,16,256]{3,2,0,1:T(8,128)(2,1)} %pad_maximum_fusion.4), channel_id=1, source_target_pairs={{128,0},{136,8},{144,16},{152,24},{160,32},{168,40},{176,48},{184,... | collective-permute-start | bytes 147464 | tf_op jit(solution)/shard_map/ppermute | solution.py:51
  35.7 15.7 %copy-start.2 = (bf16[768,512]{1,0:T(8,128)(2,1)S(1)}, bf16[768,512]{1,0:T(8,128)(2,1)}, u32[]{:S(2)}) copy-start(bf16[768,512]{1,0:T(8,128)(2,1)} %param.29) | copy-start | bytes 2359300
  38.8 4.3 %collective-permute-start.5 = (bf16[2,3,16,256]{3,2,0,1:T(8,128)(2,1)}, bf16[2,3,16,256]{3,2,0,1:T(8,128)(2,1)S(1)}, u32[]{:S(2)}, u32[]{:S(2)}) collective-permute-start(bf16[2,3,16,256]{3,2,0,1:T(8,128)(2,1)} %pad_maximum_fusion.4), channel_id=1, source_target_pairs={{192,0},{200,8},{208,16},{216,24},{224,32},{232,40},{240,48},{248,... | collective-permute-start | bytes 147464 | tf_op jit(solution)/shard_map/ppermute | solution.py:51
  48.1 1.2 copy-start.7
  48.1 1.4 copy-start.10
  50.9 134.4 %all-gather.2.cloned.1.call-start = ((), (), s32[]{:S(2)}) async-start(), calls=%async_computation.1 | async-start | bytes 4325376 | tf_op jit(solution)/shard_map/all_gather | solution.py:99
  51.4 23.8 %collective-permute-start.10 = (bf16[768,512]{1,0:T(8,128)(2,1)S(1)}, bf16[768,512]{1,0:T(8,128)(2,1)S(1)}, u32[]{:S(2)}, u32[]{:S(2)}) collective-permute-start(bf16[768,512]{1,0:T(8,128)(2,1)S(1)} %copy-done.2), channel_id=1, source_target_pairs={{0,1},{1,2},{2,3},{3,4},{4,5},{5,6},{6,7},{7,0},{8,9},{9,10},{10,1... | collective-permute-start | bytes 2359304 | tf_op jit(solution)/shard_map/ppermute | solution.py:20
  75.2 0.9 copy-start.3
  76.1 20.7 %collective-permute-start.11 = (bf16[768,512]{1,0:T(8,128)(2,1)S(1)}, bf16[768,512]{1,0:T(8,128)(2,1)}, u32[]{:S(2)}, u32[]{:S(2)}) collective-permute-start(bf16[768,512]{1,0:T(8,128)(2,1)S(1)} %collective-permute-done.10), channel_id=1, source_target_pairs={{0,1},{1,2},{2,3},{3,4},{4,5},{5,6},{6,7},{7,0},{8,9},{9,10},{10,1... | collective-permute-start | bytes 2359304 | tf_op jit(solution)/shard_map/ppermute | solution.py:20
  76.1 21.2 %collective-permute-start.14 = (bf16[768,512]{1,0:T(8,128)(2,1)S(1)}, bf16[768,512]{1,0:T(8,128)(2,1)}, u32[]{:S(2)}, u32[]{:S(2)}) collective-permute-start(bf16[768,512]{1,0:T(8,128)(2,1)S(1)} %copy-done.2), channel_id=1, source_target_pairs={{0,7},{1,0},{2,1},{3,2},{4,3},{5,4},{6,5},{7,6},{8,15},{9,8},{10,9... | collective-permute-start | bytes 2359304 | tf_op jit(solution)/shard_map/ppermute | solution.py:22
  96.8 33.1 %collective-permute-start.12 = (bf16[768,512]{1,0:T(8,128)(2,1)}, bf16[768,512]{1,0:T(8,128)(2,1)}, u32[]{:S(2)}, u32[]{:S(2)}) collective-permute-start(bf16[768,512]{1,0:T(8,128)(2,1)} %collective-permute-done.11), channel_id=1, source_target_pairs={{0,1},{1,2},{2,3},{3,4},{4,5},{5,6},{6,7},{7,0},{8,9},{9,10},{10,1... | collective-permute-start | bytes 2359304 | tf_op jit(solution)/shard_map/ppermute | solution.py:20
  97.3 56.5 %collective-permute-start.15 = (bf16[768,512]{1,0:T(8,128)(2,1)}, bf16[768,512]{1,0:T(8,128)(2,1)}, u32[]{:S(2)}, u32[]{:S(2)}) collective-permute-start(bf16[768,512]{1,0:T(8,128)(2,1)} %collective-permute-done.14), channel_id=1, source_target_pairs={{0,7},{1,0},{2,1},{3,2},{4,3},{5,4},{6,5},{7,6},{8,15},{9,8},{10,9... | collective-permute-start | bytes 2359304 | tf_op jit(solution)/shard_map/ppermute | solution.py:22
  129.9 25.9 %collective-permute-start.13 = (bf16[768,512]{1,0:T(8,128)(2,1)}, bf16[768,512]{1,0:T(8,128)(2,1)}, u32[]{:S(2)}, u32[]{:S(2)}) collective-permute-start(bf16[768,512]{1,0:T(8,128)(2,1)} %collective-permute-done.12), channel_id=1, source_target_pairs={{0,1},{1,2},{2,3},{3,4},{4,5},{5,6},{6,7},{7,0},{8,9},{9,10},{10,1... | collective-permute-start | bytes 2359304 | tf_op jit(solution)/shard_map/ppermute | solution.py:20
  134.7 10.3 %collective-permute-start.6 = (bf16[3,4,256]{2,1,0:T(4,128)(2,1)S(1)}, bf16[3,4,256]{2,1,0:T(4,128)(2,1)S(1)}, u32[]{:S(2)}, u32[]{:S(2)}) collective-permute-start(bf16[3,4,256]{2,1,0:T(4,128)(2,1)S(1)} %get-tuple-element.42), channel_id=1, source_target_pairs={{0,0},{8,32},{16,64},{24,96},{32,128},{40,160},{48,192},{56,224},{... | collective-permute-start | bytes 18440 | tf_op jit(solution)/shard_map/ppermute | solution.py:185
  137.9 11.9 %collective-permute-start.7 = (bf16[3,4,256]{2,1,0:T(4,128)(2,1)S(1)}, bf16[3,4,256]{2,1,0:T(4,128)(2,1)S(1)}, u32[]{:S(2)}, u32[]{:S(2)}) collective-permute-start(bf16[3,4,256]{2,1,0:T(4,128)(2,1)S(1)} %get-tuple-element.45), channel_id=1, source_target_pairs={{0,8},{8,40},{16,72},{24,104},{32,136},{40,168},{48,200},{56,232},... | collective-permute-start | bytes 18440 | tf_op jit(solution)/shard_map/ppermute | solution.py:185
  142.8 7.1 %collective-permute-start.8 = (bf16[3,4,256]{2,1,0:T(4,128)(2,1)S(1)}, bf16[3,4,256]{2,1,0:T(4,128)(2,1)S(1)}, u32[]{:S(2)}, u32[]{:S(2)}) collective-permute-start(bf16[3,4,256]{2,1,0:T(4,128)(2,1)S(1)} %get-tuple-element.44), channel_id=1, source_target_pairs={{0,16},{8,48},{16,80},{24,112},{32,144},{40,176},{48,208},{56,240}... | collective-permute-start | bytes 18440 | tf_op jit(solution)/shard_map/ppermute | solution.py:185
  145.0 8.8 %collective-permute-start.9 = (bf16[3,4,256]{2,1,0:T(4,128)(2,1)S(1)}, bf16[3,4,256]{2,1,0:T(4,128)(2,1)S(1)}, u32[]{:S(2)}, u32[]{:S(2)}) collective-permute-start(bf16[3,4,256]{2,1,0:T(4,128)(2,1)S(1)} %get-tuple-element.43), channel_id=1, source_target_pairs={{0,24},{8,56},{16,88},{24,120},{32,152},{40,184},{48,216},{56,248}... | collective-permute-start | bytes 18440 | tf_op jit(solution)/shard_map/ppermute | solution.py:185
  153.9 24.2 %copy-start.4 = (bf16[768,512]{1,0:T(8,128)(2,1)S(1)}, bf16[768,512]{1,0:T(8,128)(2,1)}, u32[]{:S(2)}) copy-start(bf16[768,512]{1,0:T(8,128)(2,1)} %copy-done.3) | copy-start | bytes 2359300
  153.9 16.9 %collective-permute-start.16 = (bf16[768,512]{1,0:T(8,128)(2,1)}, bf16[768,512]{1,0:T(8,128)(2,1)S(1)}, u32[]{:S(2)}, u32[]{:S(2)}) collective-permute-start(bf16[768,512]{1,0:T(8,128)(2,1)} %collective-permute-done.15), channel_id=1, source_target_pairs={{0,7},{1,0},{2,1},{3,2},{4,3},{5,4},{6,5},{7,6},{8,15},{9,8},{10,9... | collective-permute-start | bytes 2359304 | tf_op jit(solution)/shard_map/ppermute | solution.py:22
  193.6 17.8 %collective-permute-start.17 = (bf16[3,4,256]{2,1,0:T(4,128)(2,1)S(1)}, bf16[3,4,256]{2,1,0:T(4,128)(2,1)S(1)}, u32[]{:S(2)}, u32[]{:S(2)}) collective-permute-start(bf16[3,4,256]{2,1,0:T(4,128)(2,1)S(1)} %squeeze.121), channel_id=1, source_target_pairs={{0,0},{32,8},{64,16},{96,24},{128,32},{160,40},{192,48},{224,56},{... | collective-permute-start | bytes 18440 | tf_op jit(solution)/shard_map/ppermute | solution.py:196
  196.0 15.5 %collective-permute-start.18 = (bf16[3,4,256]{2,1,0:T(4,128)(2,1)S(1)}, bf16[3,4,256]{2,1,0:T(4,128)(2,1)S(1)}, u32[]{:S(2)}, u32[]{:S(2)}) collective-permute-start(bf16[3,4,256]{2,1,0:T(4,128)(2,1)S(1)} %squeeze.122), channel_id=1, source_target_pairs={{8,0},{40,8},{72,16},{104,24},{136,32},{168,40},{200,48},{232,56},... | collective-permute-start | bytes 18440 | tf_op jit(solution)/shard_map/ppermute | solution.py:196
  203.8 7.7 %collective-permute-start.19 = (bf16[3,4,256]{2,1,0:T(4,128)(2,1)S(1)}, bf16[3,4,256]{2,1,0:T(4,128)(2,1)S(1)}, u32[]{:S(2)}, u32[]{:S(2)}) collective-permute-start(bf16[3,4,256]{2,1,0:T(4,128)(2,1)S(1)} %squeeze.123), channel_id=1, source_target_pairs={{16,0},{48,8},{80,16},{112,24},{144,32},{176,40},{208,48},{240,56}... | collective-permute-start | bytes 18440 | tf_op jit(solution)/shard_map/ppermute | solution.py:196
  207.0 9.1 %collective-permute-start.20 = (bf16[3,4,256]{2,1,0:T(4,128)(2,1)S(1)}, bf16[3,4,256]{2,1,0:T(4,128)(2,1)S(1)}, u32[]{:S(2)}, u32[]{:S(2)}) collective-permute-start(bf16[3,4,256]{2,1,0:T(4,128)(2,1)S(1)} %squeeze.124), channel_id=1, source_target_pairs={{24,0},{56,8},{88,16},{120,24},{152,32},{184,40},{216,48},{248,56}... | collective-permute-start | bytes 18440 | tf_op jit(solution)/shard_map/ppermute | solution.py:196
Sparse Core Ops, SparseCore 0:
  51.0 77.6 all-reduce.1
Sparse Core Ops, SparseCore 1:
  53.9 52.4 all-gather.1
